TPU v7x, 32 devices: a whole 2x2x4 slice. The times are simulated.
32 devices in a mesh: days: 2 (over y), chan: 4 (over z), win: 4 (over x, core).
Axes of the slice: x: 2, y: 2, z: 4, core: 2. Of those that a mesh axis runs over, the one named last changes fastest.
Arguments:
- spectra: bfloat16 [2560, 32, 1024], P(('days', 'chan'), 'win'), parts along dimension 0, may hold values from -17 to 17
- pair_anchor: int32 [2048], P('chan'), may hold values from 0 to 319
- pair_offset: int32 [2048], P('chan'), may hold values from 0 to 2
- pair_partner: int32 [2048], P('chan'), may hold values from 0 to 319
- pair_count: int32 [4], P('chan'), may hold values from 1 to 512, as said below
- window_bins: int32 [64], P(('days', 'win')), parts along dimension 0, may hold values from 0 to 7
- bin_gain: float32 [8], replicated, may hold values from 0.2 to 5
Outputs:
- ref_stack: float32 [4096, 128], P(('days', 'chan')), parts along dimension 0
- restack: float32 [4096, 128], P(('days', 'chan')), parts along dimension 0
There are 2 independent parts, one for each index of `days`. A program takes and returns all parts, laid end to end along the dimension named above; an argument that names none is the same for every part. Nothing has to cross between parts.
Inputs may be any that keep to these rules, and one draw needn't show every extreme that they name: `pair_count`: each block holds from 1 to 512 live pair slots, the first ones of its slots; some block holds 512 in every draw.
All inputs are finite; a program needn't handle non-finite values.
Results may differ from a plain program's by a relative error of at most 0.0062.
Values may be sent and summed in bfloat16 or wider, within the bound.
No kernel may reach another device: no remote copies, remote signals or barrier semaphores. Data moves between devices by JAX's collectives and lax.ppermute only.
A program may use at most 128 MiB of HBM per device.

v0:
```python
import jax
import jax.numpy as jnp
from jax import lax
from jax.sharding import PartitionSpec as P

LAG = 128
EPS_POWER = 1e-05
EPS_LAG = 1e-06


def ring_neighbours(shard, axis):
    peers = lax.axis_size(axis)
    up = [(i, (i + 1) % peers) for i in range(peers)]
    down = [(j, i) for i, j in up]
    before = lax.ppermute(shard, axis, up)
    after = lax.ppermute(shard, axis, down)
    return (before, after)


def whiten(spectra):
    spectra_f = spectra.astype(jnp.float32)
    power_mean = jnp.mean(spectra_f * spectra_f, axis=-1, keepdims=True)
    return (spectra_f * lax.rsqrt(power_mean + EPS_POWER)).astype(jnp.bfloat16)


def lag_table(freq_count, lag_count):
    freq_ids = lax.broadcasted_iota(jnp.float32, (freq_count, lag_count), 0)
    lag_ids = lax.broadcasted_iota(jnp.float32, (freq_count, lag_count), 1) - lag_count // 2
    angles = 2.0 * jnp.pi / (2 * freq_count) * freq_ids * lag_ids
    norm_scale = 1.0 / jnp.sqrt(jnp.float32(freq_count))
    return jnp.concatenate(
        [jnp.cos(angles) * norm_scale, -jnp.sin(angles) * norm_scale], axis=0
    ).astype(jnp.bfloat16)


def cross_spectra(anchors, partners):
    half_width = anchors.shape[-1] // 2
    anchor_f = anchors.astype(jnp.float32)
    partner_f = partners.astype(jnp.float32)
    anchor_re = anchor_f[..., :half_width]
    anchor_im = anchor_f[..., half_width:]
    partner_re = partner_f[..., :half_width]
    partner_im = partner_f[..., half_width:]
    cross_re = anchor_re * partner_re + anchor_im * partner_im
    cross_im = anchor_im * partner_re - anchor_re * partner_im
    return jnp.concatenate([cross_re, cross_im], axis=-1).astype(jnp.bfloat16)


def window_gains(bins, gains):
    levels = lax.broadcasted_iota(jnp.int32, (bins.shape[0], gains.shape[0]), 1)
    return jnp.sum(jnp.where(bins[:, None] == levels, gains[None, :], jnp.float32(0.0)), axis=1)


def window_weights(lag_corr, ref_sum, window_gain):
    corr_f = lag_corr.astype(jnp.float32)
    inner_prod = jnp.mean(corr_f * ref_sum[:, None, :], axis=-1)
    corr_rms = jnp.sqrt(jnp.mean(corr_f * corr_f, axis=-1) + EPS_LAG)
    ref_rms = jnp.sqrt(jnp.mean(ref_sum * ref_sum, axis=-1) + EPS_LAG)
    coherence = inner_prod / (corr_rms * ref_rms[:, None])
    weights = window_gain[None, :] * jnp.exp(2.0 * coherence)
    numerator = jnp.sum(weights[:, :, None] * corr_f, axis=1)
    denominator = jnp.sum(weights, axis=1)
    return (numerator, denominator)


def select_rows(selector, rows):
    return jnp.einsum("sc,cwf->swf", selector, rows, preferred_element_type=jnp.float32)


def local(spectra, pair_anchor, pair_offset, pair_partner, pair_count, window_bins, bin_gain):
    block_chans, local_wins, spec_width = spectra.shape
    pair_slots = pair_anchor.shape[0]
    white = whiten(spectra)
    before, after = ring_neighbours(white, "chan")
    transform = lag_table(spec_width // 2, LAG)
    lag_count = transform.shape[1]
    live_count = pair_count[0]
    chan_ids = lax.broadcasted_iota(jnp.int32, (pair_slots, block_chans), 1)
    pick_anchor = (pair_anchor[:, None] == chan_ids).astype(jnp.bfloat16)
    pick_partner = pair_partner[:, None] == chan_ids
    offsets = pair_offset[:, None]
    anchors = select_rows(pick_anchor, white).astype(jnp.bfloat16)
    partners = (
        select_rows((pick_partner & (offsets == 1)).astype(jnp.bfloat16), white)
        + select_rows((pick_partner & (offsets == 0)).astype(jnp.bfloat16), before)
        + select_rows((pick_partner & (offsets == 2)).astype(jnp.bfloat16), after)
    ).astype(jnp.bfloat16)
    cross_spec = cross_spectra(anchors, partners)
    corr_full = jnp.dot(
        cross_spec.reshape(pair_slots * local_wins, spec_width),
        transform,
        preferred_element_type=jnp.float32,
    ).reshape(pair_slots, local_wins, lag_count)
    corr_all = corr_full.astype(jnp.bfloat16)
    running = jnp.sum(corr_full, axis=1)
    ref_sum = lax.psum(running, "win")
    norm_scale = jnp.sqrt(jnp.float32(local_wins * lax.axis_size("win")))
    slot_ids = lax.broadcasted_iota(jnp.int32, (pair_slots,), 0)
    live = slot_ids < live_count
    ref_stack = jnp.where(live[:, None], ref_sum / norm_scale, 0.0)
    window_gain = window_gains(window_bins, bin_gain)
    numerator, denominator = window_weights(corr_all, ref_sum, window_gain)
    numerator, denominator = lax.psum((numerator, denominator), "win")
    restack = jnp.where(live[:, None], norm_scale * numerator / denominator[:, None], 0.0)
    return (ref_stack, restack)


def solution(mesh):
    in_specs = (
        P(("days", "chan"), "win", None),
        P("chan"),
        P("chan"),
        P("chan"),
        P("chan"),
        P(("days", "win")),
        P(),
    )
    out_specs = (P(("days", "chan"), None), P(("days", "chan"), None))
    return jax.shard_map(local, mesh=mesh, in_specs=in_specs, out_specs=out_specs, check_vma=False)
```

profile of v0, /device:TPU:0, one launch (start us, length us, event | category | flops | bytes accessed | tf_op | source)
XLA Modules:
  0.0 373.9 jit_solution(18302945717183395102)
XLA Ops:
  7.2 0.0 copy-start.4
  7.2 0.0 copy-start.3
  7.2 0.0 all-reduce.3.cloned.1.call-start
  7.2 0.0 copy-start
  7.2 8.1 %fusion = f32[320,8]{0,1:T(8,128)S(1)} fusion(bf16[320,8,1024]{2,1,0:T(8,128)(2,1)} %param.7), kind=kLoop, calls=%fused_computation.3 | loop fusion | flops 7861760 | bytes 5253120 | tf_op jit(solution)/shard_map/reduce_sum | solution.py:22
  15.4 0.0 copy-done
  15.4 4.2 %fusion.1 = bf16[320,8,1024]{2,0,1:T(8,128)(2,1)S(1)} fusion(f32[320,8]{0,1:T(8,128)S(1)} %add_rsqrt_fusion, bf16[320,8,1024]{2,1,0:T(8,128)(2,1)S(1)} %copy-done), kind=kLoop, calls=%fused_computation.4 | loop fusion | flops 7864320 | bytes 10496000 | tf_op jit(solution)/shard_map/convert_element_type | solution.py:23
  19.5 3.1 collective-permute-start
  22.6 2.3 collective-permute-start.1
  25.6 0.0 copy-done.4
  25.6 1.1 fusion.31
  26.7 0.0 copy-done.3
  26.7 0.0 copy-start.2
  26.7 8.2 %convert_convert_fusion = f32[512,8,1024]{2,0,1:T(8,128)} fusion(bf16[320,8,1024]{2,0,1:T(8,128)(2,1)S(1)} %fusion.1, s32[512]{0:T(512)S(1)} %copy-done.3), kind=kOutput, calls=%fused_computation.11 | convolution fusion | flops 2692907008 | bytes 22022144 | tf_op jit(solution)/shard_map/sc,cwf->swf/dot_general | solution.py:67
  35.0 0.0 copy-done.2
  35.0 8.2 %fusion.16 = f32[512,8,1024]{2,0,1:T(8,128)} fusion(bf16[320,8,1024]{2,0,1:T(8,128)(2,1)S(1)} %fusion.1, s32[512]{0:T(512)S(1)} %copy-done.2, pred[512]{0:T(512)(128)(4,1)S(1)} %get-tuple-element.17), kind=kOutput, calls=%fused_computation.26 | convolution fusion | flops 2684682240 | bytes 22022656 | tf_op jit(solution)/shard_map/sc,cwf->swf/dot_general | solution.py:67
  43.2 95.4 %collective-permute-done = bf16[320,8,1024]{2,0,1:T(8,128)(2,1)S(1)} collective-permute-done((bf16[320,8,1024]{2,0,1:T(8,128)(2,1)S(1)}, bf16[320,8,1024]{2,0,1:T(8,128)(2,1)S(1)}, u32[]{:S(2)}, u32[]{:S(2)}) %collective-permute-start) | collective-permute-done | bytes 5242912 | tf_op jit(solution)/shard_map/ppermute | solution.py:15
  138.6 8.2 %fusion.19 = f32[512,8,1024]{2,0,1:T(8,128)} fusion(bf16[320,8,1024]{2,0,1:T(8,128)(2,1)S(1)} %collective-permute-done, s32[512]{0:T(512)S(1)} %copy-done.2, pred[512]{0:T(512)(128)(4,1)S(1)} %get-tuple-element.18), kind=kOutput, calls=%fused_computation.28 | convolution fusion | flops 2684682240 | bytes 22022656 | tf_op jit(solution)/shard_map/sc,cwf->swf/dot_general | solution.py:67
  146.7 102.7 %collective-permute-done.1 = bf16[320,8,1024]{2,0,1:T(8,128)(2,1)S(1)} collective-permute-done((bf16[320,8,1024]{2,0,1:T(8,128)(2,1)S(1)}, bf16[320,8,1024]{2,0,1:T(8,128)(2,1)S(1)}, u32[]{:S(2)}, u32[]{:S(2)}) %collective-permute-start.1) | collective-permute-done | bytes 5242912 | tf_op jit(solution)/shard_map/ppermute | solution.py:16
  249.5 0.0 copy-start.1
  249.5 2.4 copy-done.1
  251.9 20.8 %fusion.6 = f32[512,8,1024]{2,0,1:T(8,128)} fusion(bf16[320,8,1024]{2,0,1:T(8,128)(2,1)} %copy-done.1, f32[512,8,1024]{2,0,1:T(8,128)} %fusion.16, f32[512,8,1024]{2,0,1:T(8,128)} %fusion.19, s32[512]{0:T(512)S(1)} %copy-done.2, pred[512]{0:T(512)(128)(4,1)S(1)} %get-tuple-element.16), kind=kOutput, calls=%fused_computation.12 | convolution fusion | flops 2701459456 | bytes 55577088 | tf_op jit(solution)/shard_map/sc,cwf->swf/dot_general | solution.py:67
  272.6 13.0 %add_convert_fusion.1 = (bf16[512,8,512]{2,0,1:T(8,128)(2,1)S(1)}, bf16[512,8,512]{2,0,1:T(8,128)(2,1)S(1)}) fusion(f32[512,8,1024]{2,0,1:T(8,128)} %fusion.6, f32[512,8,1024]{2,0,1:T(8,128)} %convert_convert_fusion), kind=kLoop, calls=%fused_computation.10 | loop fusion | flops 16777216 | bytes 41943040 | tf_op jit(solution)/shard_map/convert.2
  285.7 0.0 copy-start.5
  285.7 0.0 copy-start.6
  285.7 3.7 %fusion.39 = (f32[512,128]{0,1:T(8,128)}, bf16[512,8,128]{0,2,1:T(8,128)(2,1)S(1)}) fusion(bf16[512,128]{0,1:T(8,128)(2,1)S(1)} %get-tuple-element.15, bf16[512,128]{0,1:T(8,128)(2,1)S(1)} %get-tuple-element.14, bf16[512,8,512]{2,0,1:T(8,128)(2,1)S(1)} %get-tuple-element.11, bf16[512,8,512]{2,0,1:T(8,128)(2,1)S(1)} %get-tuple-element.10), kind=kOutput, calls=%fused_computation.63 | convolution fusion | flops 1092026368 | bytes 9961472 | tf_op jit(solution)/shard_map/dot_general | solution.py:89
  289.5 0.0 all-reduce.3.cloned.1.call-update
  289.5 0.0 all-reduce.5.cloned.1.call-start
  289.5 0.0 copy-done.5
  289.6 0.0 copy-done.6
  289.6 0.2 select_reduce_fusion
  289.7 40.0 %all-reduce.3.cloned.1.call-done = f32[512,128]{0,1:T(8,128)} async-done(((f32[512,128]{0,1:T(8,128)}), f32[512,128]{0,1:T(8,128)}) %all-reduce.3.cloned.1.call-update) | async-done | bytes 262160 | tf_op jit(solution)/shard_map/psum | solution.py:96
  329.7 1.0 multiply_reduce_fusion
  330.8 1.4 fusion.7
  332.1 0.1 fusion.38
  332.2 0.9 fusion.9
  333.1 0.0 all-reduce.5.cloned.1.call-update
  333.1 0.8 copy.15
  334.0 5.7 %psum.23 = f32[512]{0:T(512)S(1)} all-reduce(f32[512]{0:T(512)S(1)} %get-tuple-element.8), channel_id=1, replica_groups=mesh['days'=2,'chan'=4,'win'=4] {'win'}, use_global_device_ids=true, to_apply=%region_10.11 | all-reduce | flops 512 | bytes 4096 | tf_op jit(solution)/shard_map/psum | solution.py:103
  339.7 25.6 %all-reduce.5.cloned.1.call-done = f32[512,128]{0,1:T(8,128)} async-done(((f32[512,128]{0,1:T(8,128)}), f32[512,128]{0,1:T(8,128)}) %all-reduce.5.cloned.1.call-update) | async-done | bytes 262160 | tf_op jit(solution)/shard_map/psum | solution.py:103
  365.3 1.0 divide_select_fusion
  366.3 0.8 copy.16
  (6 shorter events, 0.0 us)
Async XLA Ops:
  7.2 18.4 %copy-start.4 = (s32[512]{0:T(512)S(1)}, s32[512]{0:T(512)}, u32[]{:S(2)}) copy-start(s32[512]{0:T(512)} %param.9) | copy-start | bytes 6148
  7.2 19.6 %copy-start.3 = (s32[512]{0:T(512)S(1)}, s32[512]{0:T(512)}, u32[]{:S(2)}) copy-start(s32[512]{0:T(512)} %param.8) | copy-start | bytes 6148
  7.2 322.6 %all-reduce.3.cloned.1.call-start = ((), (), s32[]{:S(2)}) async-start(), calls=%async_computation | async-start | bytes 524288 | tf_op jit(solution)/shard_map/psum | solution.py:96
  7.2 8.1 %copy-start = (bf16[320,8,1024]{2,1,0:T(8,128)(2,1)S(1)}, bf16[320,8,1024]{2,1,0:T(8,128)(2,1)}, u32[]{:S(2)}) copy-start(bf16[320,8,1024]{2,1,0:T(8,128)(2,1)} %param.7) | copy-start | bytes 15728644
  19.5 119.0 %collective-permute-start = (bf16[320,8,1024]{2,0,1:T(8,128)(2,1)S(1)}, bf16[320,8,1024]{2,0,1:T(8,128)(2,1)S(1)}, u32[]{:S(2)}, u32[]{:S(2)}) collective-permute-start(bf16[320,8,1024]{2,0,1:T(8,128)(2,1)S(1)} %fusion.1), channel_id=1, source_target_pairs={{0,4},{4,8},{8,12},{12,0},{1,5},{5,9},{9,13},{13,1},{2,6},{6,10},{... | collective-permute-start | bytes 15728648 | tf_op jit(solution)/shard_map/ppermute | solution.py:15
  22.6 226.9 %collective-permute-start.1 = (bf16[320,8,1024]{2,0,1:T(8,128)(2,1)S(1)}, bf16[320,8,1024]{2,0,1:T(8,128)(2,1)S(1)}, u32[]{:S(2)}, u32[]{:S(2)}) collective-permute-start(bf16[320,8,1024]{2,0,1:T(8,128)(2,1)S(1)} %fusion.1), channel_id=1, source_target_pairs={{4,0},{8,4},{12,8},{0,12},{5,1},{9,5},{13,9},{1,13},{6,2},{10,6},{... | collective-permute-start | bytes 15728648 | tf_op jit(solution)/shard_map/ppermute | solution.py:16
  26.7 8.2 %copy-start.2 = (s32[512]{0:T(512)S(1)}, s32[512]{0:T(512)}, u32[]{:S(2)}) copy-start(s32[512]{0:T(512)} %param.10) | copy-start | bytes 6148
  249.5 2.4 copy-start.1
  285.7 3.9 %copy-start.5 = (f32[8]{0:T(128)S(1)}, f32[8]{0:T(128)}, u32[]{:S(2)}) copy-start(f32[8]{0:T(128)} %param.13) | copy-start | bytes 100
  285.7 3.9 %copy-start.6 = (s32[8]{0:T(128)S(1)}, s32[8]{0:T(128)}, u32[]{:S(2)}) copy-start(s32[8]{0:T(128)} %param.12) | copy-start | bytes 100
  289.5 75.8 %all-reduce.5.cloned.1.call-start = ((), (), s32[]{:S(2)}) async-start(), calls=%async_computation.1 | async-start | bytes 524288 | tf_op jit(solution)/shard_map/psum | solution.py:103
Sparse Core Ops, SparseCore 0:
  289.6 40.0 all-reduce.2
  333.3 31.9 all-reduce.4
where the time goes:
time: 374 us
  waiting for transfers between devices  264 us (71%)
  matrix products  49.1 us (13%)
  other arithmetic  31 us (8%)
  between operations  14.8 us (4%)
  blocking collectives  5.73 us (2%)
  starting transfers between devices  5.43 us (1%)
  local copies, waits for them, and re-layouts  4.09 us (1%)
    ppermute x1, waiting for transfers between devices, ring_neighbours(): after = lax.ppermute(shard, axis, down)  103 us
    ppermute x1, waiting for transfers between devices, ring_neighbours(): before = lax.ppermute(shard, axis, up)  95.4 us
    dot_general x4, matrix products, select_rows(): jnp.einsum('sc,cwf->swf', selector, rows, preferred_element_type=jnp.floa...  45.4 us
    psum x1, waiting for transfers between devices, local(): ref_sum = lax.psum(running, 'win')  40 us
    psum x1, waiting for transfers between devices, local(): numerator, denominator = lax.psum((numerator, denominator), 'win')  25.6 us
    another operation x2, other arithmetic  14.2 us
    reduce_sum x1, other arithmetic, whiten(): power_mean = jnp.mean(spectra_f * spectra_f, axis=-1, keepdims=True)  8.1 us
  transfers between devices with their start and end apart: 4, of which 4 were waited for; matrix products, arithmetic and copies ran while one was open for 7% of the time, Pallas kernels for 0%

commit v1 on v0

--- a/solution.py
+++ b/solution.py
@@ -93,7 +93,8 @@
     ).reshape(pair_slots, local_wins, lag_count)
     corr_all = corr_full.astype(jnp.bfloat16)
     running = jnp.sum(corr_full, axis=1)
-    ref_sum = lax.psum(running, "win")
+    parts = lax.all_gather(running, "win", axis=0, tiled=False)
+    ref_sum = parts.sum(axis=0)
     norm_scale = jnp.sqrt(jnp.float32(local_wins * lax.axis_size("win")))
     slot_ids = lax.broadcasted_iota(jnp.int32, (pair_slots,), 0)
     live = slot_ids < live_count

time: 374 us -> 360 us (0.963)
  waiting for transfers between devices: 264 us -> 248 us
    psum x1 -> x0, waiting for transfers between devices: 40 us -> none  [local(): ref_sum = lax.psum(running, 'win')]
    all_gather x0 -> x1, waiting for transfers between devices: none -> 24.1 us  [local(): parts = lax.all_gather(running, 'win', axis=0, tiled=False)]
where the time goes in v1:
time: 360 us; the launch traced here: 359 us
  waiting for transfers between devices  248 us (69%)
  matrix products  49.1 us (14%)
  other arithmetic  29.7 us (8%)
  between operations  14.8 us (4%)
  local copies, waits for them, and re-layouts  6.02 us (2%)
  blocking collectives  5.86 us (2%)
  starting transfers between devices  5.43 us (2%)
    ppermute x1, waiting for transfers between devices, ring_neighbours(): after = lax.ppermute(shard, axis, down)  103 us
    ppermute x1, waiting for transfers between devices, ring_neighbours(): before = lax.ppermute(shard, axis, up)  96 us
    dot_general x4, matrix products, select_rows(): jnp.einsum('sc,cwf->swf', selector, rows, preferred_element_type=jnp.floa...  45.4 us
    psum x1, waiting for transfers between devices, local(): numerator, denominator = lax.psum((numerator, denominator), 'win')  25.4 us
    all_gather x1, waiting for transfers between devices, local(): parts = lax.all_gather(running, 'win', axis=0, tiled=False)  24.1 us
    another operation x2, other arithmetic  14.2 us
    reduce_sum x1, other arithmetic, whiten(): power_mean = jnp.mean(spectra_f * spectra_f, axis=-1, keepdims=True)  8.1 us
  transfers between devices with their start and end apart: 4, of which 4 were waited for; matrix products, arithmetic and copies ran while one was open for 7% of the time, Pallas kernels for 0%

profile of v1, /device:TPU:0, one launch (start us, length us, event | category | flops | bytes accessed | tf_op | source)
XLA Modules:
  0.0 359.4 jit_solution(1434552448215055625)
XLA Ops:
  7.2 0.0 copy-start.4
  7.2 0.0 copy-start.3
  7.2 0.0 all-gather.3.cloned.1.call-start
  7.2 0.0 copy-start
  7.2 8.1 %fusion = f32[320,8]{0,1:T(8,128)S(1)} fusion(bf16[320,8,1024]{2,1,0:T(8,128)(2,1)} %param.7), kind=kLoop, calls=%fused_computation.3 | loop fusion | flops 7861760 | bytes 5253120 | tf_op jit(solution)/shard_map/reduce_sum | solution.py:22
  15.4 0.0 copy-done
  15.4 4.2 %fusion.1 = bf16[320,8,1024]{2,0,1:T(8,128)(2,1)S(1)} fusion(f32[320,8]{0,1:T(8,128)S(1)} %add_rsqrt_fusion, bf16[320,8,1024]{2,1,0:T(8,128)(2,1)S(1)} %copy-done), kind=kLoop, calls=%fused_computation.4 | loop fusion | flops 7864320 | bytes 10496000 | tf_op jit(solution)/shard_map/convert_element_type | solution.py:23
  19.5 3.1 collective-permute-start
  22.6 2.3 collective-permute-start.1
  24.9 0.0 copy-done.4
  24.9 1.1 fusion.31
  26.1 0.0 copy-done.3
  26.1 0.0 copy-start.2
  26.1 8.2 %convert_convert_fusion = f32[512,8,1024]{2,0,1:T(8,128)} fusion(bf16[320,8,1024]{2,0,1:T(8,128)(2,1)S(1)} %fusion.1, s32[512]{0:T(512)S(1)} %copy-done.3), kind=kOutput, calls=%fused_computation.11 | convolution fusion | flops 2692907008 | bytes 22022144 | tf_op jit(solution)/shard_map/sc,cwf->swf/dot_general | solution.py:67
  34.3 0.0 copy-done.2
  34.3 8.2 %fusion.16 = f32[512,8,1024]{2,0,1:T(8,128)} fusion(bf16[320,8,1024]{2,0,1:T(8,128)(2,1)S(1)} %fusion.1, s32[512]{0:T(512)S(1)} %copy-done.2, pred[512]{0:T(512)(128)(4,1)S(1)} %get-tuple-element.17), kind=kOutput, calls=%fused_computation.26 | convolution fusion | flops 2684682240 | bytes 22022656 | tf_op jit(solution)/shard_map/sc,cwf->swf/dot_general | solution.py:67
  42.5 96.0 %collective-permute-done = bf16[320,8,1024]{2,0,1:T(8,128)(2,1)S(1)} collective-permute-done((bf16[320,8,1024]{2,0,1:T(8,128)(2,1)S(1)}, bf16[320,8,1024]{2,0,1:T(8,128)(2,1)S(1)}, u32[]{:S(2)}, u32[]{:S(2)}) %collective-permute-start) | collective-permute-done | bytes 5242912 | tf_op jit(solution)/shard_map/ppermute | solution.py:15
  138.6 8.2 %fusion.19 = f32[512,8,1024]{2,0,1:T(8,128)} fusion(bf16[320,8,1024]{2,0,1:T(8,128)(2,1)S(1)} %collective-permute-done, s32[512]{0:T(512)S(1)} %copy-done.2, pred[512]{0:T(512)(128)(4,1)S(1)} %get-tuple-element.18), kind=kOutput, calls=%fused_computation.28 | convolution fusion | flops 2684682240 | bytes 22022656 | tf_op jit(solution)/shard_map/sc,cwf->swf/dot_general | solution.py:67
  146.7 102.7 %collective-permute-done.1 = bf16[320,8,1024]{2,0,1:T(8,128)(2,1)S(1)} collective-permute-done((bf16[320,8,1024]{2,0,1:T(8,128)(2,1)S(1)}, bf16[320,8,1024]{2,0,1:T(8,128)(2,1)S(1)}, u32[]{:S(2)}, u32[]{:S(2)}) %collective-permute-start.1) | collective-permute-done | bytes 5242912 | tf_op jit(solution)/shard_map/ppermute | solution.py:16
  249.5 0.0 copy-start.1
  249.5 2.4 copy-done.1
  251.9 20.8 %fusion.6 = f32[512,8,1024]{2,0,1:T(8,128)} fusion(bf16[320,8,1024]{2,0,1:T(8,128)(2,1)} %copy-done.1, f32[512,8,1024]{2,0,1:T(8,128)} %fusion.16, f32[512,8,1024]{2,0,1:T(8,128)} %fusion.19, s32[512]{0:T(512)S(1)} %copy-done.2, pred[512]{0:T(512)(128)(4,1)S(1)} %get-tuple-element.16), kind=kOutput, calls=%fused_computation.12 | convolution fusion | flops 2701459456 | bytes 55577088 | tf_op jit(solution)/shard_map/sc,cwf->swf/dot_general | solution.py:67
  272.6 13.0 %add_convert_fusion.1 = (bf16[512,8,512]{2,0,1:T(8,128)(2,1)S(1)}, bf16[512,8,512]{2,0,1:T(8,128)(2,1)S(1)}) fusion(f32[512,8,1024]{2,0,1:T(8,128)} %fusion.6, f32[512,8,1024]{2,0,1:T(8,128)} %convert_convert_fusion), kind=kLoop, calls=%fused_computation.10 | loop fusion | flops 16777216 | bytes 41943040 | tf_op jit(solution)/shard_map/convert.2
  285.7 0.0 copy-start.5
  285.7 0.0 copy-start.6
  285.7 3.7 %fusion.39 = (f32[512,128]{0,1:T(8,128)}, bf16[512,8,128]{0,2,1:T(8,128)(2,1)S(1)}) fusion(bf16[512,128]{0,1:T(8,128)(2,1)S(1)} %get-tuple-element.15, bf16[512,128]{0,1:T(8,128)(2,1)S(1)} %get-tuple-element.14, bf16[512,8,512]{2,0,1:T(8,128)(2,1)S(1)} %get-tuple-element.11, bf16[512,8,512]{2,0,1:T(8,128)(2,1)S(1)} %get-tuple-element.10), kind=kOutput, calls=%fused_computation.63 | convolution fusion | flops 1092026368 | bytes 9961472 | tf_op jit(solution)/shard_map/dot_general | solution.py:89
  289.5 0.0 all-gather.3.cloned.1.call-update
  289.5 0.0 all-reduce.2.cloned.1.call-start
  290.2 0.0 copy-done.5
  290.2 0.0 copy-done.6
  290.2 0.2 select_reduce_fusion
  290.4 24.1 %all-gather.3.cloned.1.call-done = f32[2048,128]{0,1:T(8,128)} async-done(((f32[512,128]{0,1:T(8,128)}), f32[2048,128]{0,1:T(8,128)}) %all-gather.3.cloned.1.call-update) | async-done | bytes 1048592 | tf_op jit(solution)/shard_map/all_gather | solution.py:96
  314.5 1.9 reshape.80
  316.5 0.6 reduce_sum.83
  317.1 0.4 fusion.7
  317.5 0.1 multiply_reduce_fusion
  317.6 0.1 fusion.38
  317.7 0.9 fusion.9
  318.6 0.0 all-reduce.2.cloned.1.call-update
  318.6 0.8 copy.15
  319.4 5.9 %psum.15 = f32[512]{0:T(512)S(1)} all-reduce(f32[512]{0:T(512)S(1)} %get-tuple-element.8), channel_id=1, replica_groups=mesh['days'=2,'chan'=4,'win'=4] {'win'}, use_global_device_ids=true, to_apply=%region_10.11 | all-reduce | flops 512 | bytes 4096 | tf_op jit(solution)/shard_map/psum | solution.py:104
  325.3 25.4 %all-reduce.2.cloned.1.call-done = f32[512,128]{0,1:T(8,128)} async-done(((f32[512,128]{0,1:T(8,128)}), f32[512,128]{0,1:T(8,128)}) %all-reduce.2.cloned.1.call-update) | async-done | bytes 262160 | tf_op jit(solution)/shard_map/psum | solution.py:104
  350.7 1.0 divide_select_fusion
  351.7 0.8 copy.16
  (6 shorter events, 0.0 us)
Async XLA Ops:
  7.2 17.7 %copy-start.4 = (s32[512]{0:T(512)S(1)}, s32[512]{0:T(512)}, u32[]{:S(2)}) copy-start(s32[512]{0:T(512)} %param.9) | copy-start | bytes 6148
  7.2 18.9 %copy-start.3 = (s32[512]{0:T(512)S(1)}, s32[512]{0:T(512)}, u32[]{:S(2)}) copy-start(s32[512]{0:T(512)} %param.8) | copy-start | bytes 6148
  7.2 307.4 %all-gather.3.cloned.1.call-start = ((), (), s32[]{:S(2)}) async-start(), calls=%async_computation.1 | async-start | bytes 1310720 | tf_op jit(solution)/shard_map/all_gather | solution.py:96
  7.2 8.1 %copy-start = (bf16[320,8,1024]{2,1,0:T(8,128)(2,1)S(1)}, bf16[320,8,1024]{2,1,0:T(8,128)(2,1)}, u32[]{:S(2)}) copy-start(bf16[320,8,1024]{2,1,0:T(8,128)(2,1)} %param.7) | copy-start | bytes 15728644
  19.5 119.0 %collective-permute-start = (bf16[320,8,1024]{2,0,1:T(8,128)(2,1)S(1)}, bf16[320,8,1024]{2,0,1:T(8,128)(2,1)S(1)}, u32[]{:S(2)}, u32[]{:S(2)}) collective-permute-start(bf16[320,8,1024]{2,0,1:T(8,128)(2,1)S(1)} %fusion.1), channel_id=1, source_target_pairs={{0,4},{4,8},{8,12},{12,0},{1,5},{5,9},{9,13},{13,1},{2,6},{6,10},{... | collective-permute-start | bytes 15728648 | tf_op jit(solution)/shard_map/ppermute | solution.py:15
  22.6 226.9 %collective-permute-start.1 = (bf16[320,8,1024]{2,0,1:T(8,128)(2,1)S(1)}, bf16[320,8,1024]{2,0,1:T(8,128)(2,1)S(1)}, u32[]{:S(2)}, u32[]{:S(2)}) collective-permute-start(bf16[320,8,1024]{2,0,1:T(8,128)(2,1)S(1)} %fusion.1), channel_id=1, source_target_pairs={{4,0},{8,4},{12,8},{0,12},{5,1},{9,5},{13,9},{1,13},{6,2},{10,6},{... | collective-permute-start | bytes 15728648 | tf_op jit(solution)/shard_map/ppermute | solution.py:16
  26.1 8.2 %copy-start.2 = (s32[512]{0:T(512)S(1)}, s32[512]{0:T(512)}, u32[]{:S(2)}) copy-start(s32[512]{0:T(512)} %param.10) | copy-start | bytes 6148
  249.5 2.4 copy-start.1
  285.7 4.5 %copy-start.5 = (f32[8]{0:T(128)S(1)}, f32[8]{0:T(128)}, u32[]{:S(2)}) copy-start(f32[8]{0:T(128)} %param.13) | copy-start | bytes 100
  285.7 4.5 %copy-start.6 = (s32[8]{0:T(128)S(1)}, s32[8]{0:T(128)}, u32[]{:S(2)}) copy-start(s32[8]{0:T(128)} %param.12) | copy-start | bytes 100
  289.5 61.3 %all-reduce.2.cloned.1.call-start = ((), (), s32[]{:S(2)}) async-start(), calls=%async_computation | async-start | bytes 524288 | tf_op jit(solution)/shard_map/psum | solution.py:104
Sparse Core Ops, SparseCore 0:
  289.6 24.8 all-gather.2
  318.7 31.9 all-reduce.1
